TPU v7x, 256 devices: a whole 4x4x8 slice. The times are simulated.
256 devices in a mesh: section: 8 (over z), joint: 32 (over y, x, core).
Axes of the slice: x: 4, y: 4, z: 8, core: 2. Of those that a mesh axis runs over, the one named last changes fastest.
Arguments:
- encoder_rows: bfloat16 [32, 1024, 1536], P('joint', 'section'), may hold values from -6 to 6
- up_weight: bfloat16 [1536, 3072], P(None, 'section'), may hold values from -0.15625 to 0.15625
- down_weight: bfloat16 [3072, 1536], P('section'), may hold values from -0.109375 to 0.109375
- encoder_proj: bfloat16 [1536, 640], replicated, may hold values from -0.15625 to 0.15625
- embedding: bfloat16 [4096, 640], P('joint'), may hold values from -6 to 6
- conv_taps: float32 [2, 640], replicated, may hold values from -3 to 3
- decoder_proj: bfloat16 [640, 640], replicated, may hold values from -0.25 to 0.25
- output_proj: bfloat16 [640, 4096], replicated, may hold values from -0.5 to 0.5
- output_bias: float32 [4096], replicated, may hold values from -6 to 6
- frame_lengths: int32 [32], replicated, may hold values from 1 to 1024, 20480 in all
- label_lengths: int32 [32], replicated, may hold values from 1 to 3, 48 in all
- label_ids: int32 [32, 3], replicated, may hold values from 1 to 4095
- owner_index: int32 [32], replicated, may hold values from 0 to 31, each once
Outputs:
- enc_grad: bfloat16 [32, 1024, 1536], P('joint', 'section')
- up_grad: float32 [1536, 3072], P('joint', 'section')
- down_grad: float32 [3072, 1536], P('section', 'joint')
- pred_grad: float32 [32, 4, 640], P('joint', None, 'section')
Inputs may be any that keep to these rules, and one draw needn't show every extreme that they name: `owner_index`: every joint owner receives exactly one utterance. `frame_lengths`: the longest utterance uses all 1024 frames. `label_lengths`: the longest label sequence has 3 labels. `label_ids`: never the blank token 0.
All inputs are finite; a program needn't handle non-finite values.
Results may differ from a plain program's by a relative error of at most 0.013.
Values may be sent and summed in bfloat16 or wider, within the bound.
No kernel may reach another device: no remote copies, remote signals or barrier semaphores. Data moves between devices by JAX's collectives and lax.ppermute only.
A program may use at most 128 MiB of HBM per device.

v0:
```python
import jax
import jax.numpy as jnp
from jax import lax
from jax.sharding import PartitionSpec as P

NEG_BIG = -1000000000.0


def partner_2(block, axis, bit):
    count = lax.axis_size(axis)
    route = []
    for low in range(count):
        high = low | 1 << bit
        if high != low and high < count:
            route += [(low, high), (high, low)]
    return lax.ppermute(block, axis, route)


def from_behind(value, axis, steps):
    count = lax.axis_size(axis)
    initial, last = (max(0, -steps), min(count, count - steps))
    return lax.ppermute(value, axis, [(source, source + steps) for source in range(initial, last)])


def layer_norm(values):
    average = jnp.mean(values, axis=-1, keepdims=True)
    centered = values - average
    variance = jnp.mean(centered * centered, axis=-1, keepdims=True)
    inv_scale = lax.rsqrt(variance + 1e-05)
    return (centered * inv_scale, inv_scale)


def lower_paths(label_row):
    partial_sums = jnp.concatenate([jnp.zeros((1,), jnp.float32), jnp.cumsum(label_row)])
    places = partial_sums.shape[0]
    row_ids = lax.broadcasted_iota(jnp.int32, (places, places), 0)
    col_ids = lax.broadcasted_iota(jnp.int32, (places, places), 1)
    return jnp.where(col_ids <= row_ids, partial_sums[:, None] - partial_sums[None, :], NEG_BIG)


def advance(vector, blank_row, label_row, active):
    moved = blank_row + jax.nn.logsumexp(lower_paths(label_row) + vector[None, :], axis=1)
    return jnp.where(active, moved, vector)


def run_block(vector, blank_score, label_score, active):

    def run_one_frame(carried, inputs):
        blank_row, label_row, live_flag = inputs
        return (advance(carried, blank_row, label_row, live_flag), None)

    return lax.scan(run_one_frame, vector, (blank_score, label_score, active))[0]


def block_matrix(blank_score, label_score, active):
    places = blank_score.shape[1]
    row_ids = lax.broadcasted_iota(jnp.int32, (places, places), 0)
    col_ids = lax.broadcasted_iota(jnp.int32, (places, places), 1)
    identity_map = jnp.where(row_ids == col_ids, 0.0, NEG_BIG)

    def block_one_frame(carried, inputs):
        blank_row, label_row, live_flag = inputs
        moved = blank_row[:, None] + jax.nn.logsumexp(
            lower_paths(label_row)[:, :, None] + carried[None, :, :], axis=1
        )
        return (jnp.where(live_flag, moved, carried), None)

    return lax.scan(block_one_frame, identity_map, (blank_score, label_score, active))[0]


def log_apply(transfer, vector):
    return jax.nn.logsumexp(transfer + vector[None, :], axis=1)


def log_apply_back(transfer, vector):
    return jax.nn.logsumexp(transfer + vector[:, None], axis=0)


def joint_forward(frame_part, pred_here, label_row_ids, output_proj, output_bias):
    joined = jnp.tanh(frame_part.astype(jnp.float32)[:, None, :] + pred_here[None, :, :]).astype(
        jnp.bfloat16
    )
    frames_here, places, joint_width = joined.shape
    logits = (
        jnp.dot(
            joined.reshape(frames_here * places, joint_width),
            output_proj,
            preferred_element_type=jnp.float32,
        )
        + output_bias
    )
    logits = logits.reshape(frames_here, places, -1)
    exponent = jnp.exp(logits)
    denominator = jnp.sum(exponent, axis=-1, keepdims=True)
    log_total = jnp.log(denominator)[:, :, 0]
    blank_score = logits[:, :, 0] - log_total
    index_grid = jnp.broadcast_to(label_row_ids[None, :, None], (frames_here, places - 1, 1))
    picked = jnp.take_along_axis(logits[:, :-1, :], index_grid, axis=2)[:, :, 0]
    label_score = picked - log_total[:, :-1]
    posterior = exponent / denominator
    return (joined, posterior, blank_score, label_score)


def joint_backward(blank_grad, label_grad, label_row_ids, joined, posterior, output_proj):
    frames_here, places, vocab_size = posterior.shape
    label_full = jnp.pad(label_grad, ((0, 0), (0, 1)))
    weight_sum = blank_grad + label_full
    token_full = jnp.concatenate([label_row_ids, jnp.full((1,), -1, jnp.int32)])
    vocab_iota = lax.broadcasted_iota(jnp.int32, (1, 1, vocab_size), 2)
    blank_term = jnp.where(vocab_iota == 0, blank_grad[:, :, None], 0.0)
    label_term = jnp.where(vocab_iota == token_full[None, :, None], label_full[:, :, None], 0.0)
    logit_grad = -posterior * weight_sum[:, :, None] + blank_term + label_term
    logit_grad = logit_grad.astype(jnp.bfloat16).reshape(frames_here * places, vocab_size)
    joined_grad = lax.dot_general(
        logit_grad, output_proj, (((1,), (1,)), ((), ())), preferred_element_type=jnp.float32
    )
    joined_vals = joined.astype(jnp.float32).reshape(frames_here * places, -1)
    inner_grad = (joined_grad * (1.0 - joined_vals * joined_vals)).reshape(frames_here, places, -1)
    frame_part_grad = jnp.sum(inner_grad, axis=1).astype(jnp.bfloat16)
    pred_part_grad = jnp.sum(inner_grad, axis=0)
    return (frame_part_grad, pred_part_grad)


def network_sections(count):
    sections = []
    block_size = 2
    while block_size <= count:
        stride = block_size // 2
        while stride >= 1:
            sections.append((block_size, stride))
            stride = stride // 2
        block_size = block_size * 2
    return sections


def sort_section(keys, block_size, stride, device_id):
    count = keys.shape[0]
    position = jnp.arange(count, dtype=jnp.int32)
    partner = position ^ stride
    partner_keys = keys[partner]
    rising = position & block_size == 0
    lower_side = position < partner
    keep_small = lower_side == rising
    new_keys = jnp.where(
        keep_small, jnp.minimum(keys, partner_keys), jnp.maximum(keys, partner_keys)
    )
    takes = new_keys[device_id] != keys[device_id]
    return (new_keys, takes)


def route_owner(payload, keys, device_id, count):
    for block_size, stride in network_sections(count):
        keys, takes = sort_section(keys, block_size, stride, device_id)
        other = partner_2(payload, "joint", stride.bit_length() - 1)
        payload = jnp.where(takes, other, payload)
    return payload


def route_holder(payload, keys, device_id, count):
    for block_size, stride in network_sections(count):
        keys, takes = sort_section(keys, block_size, stride, device_id)
        other = partner_2(payload, "joint", stride.bit_length() - 1)
        payload = jnp.where(takes, other, payload)
    return payload


def on_device(
    encoder_rows,
    up_weight,
    down_weight,
    encoder_proj,
    embedding,
    conv_taps,
    decoder_proj,
    output_proj,
    output_bias,
    frame_lengths,
    label_lengths,
    label_ids,
    owner_index,
):
    section_count = lax.axis_size("section")
    joint_count = lax.axis_size("joint")
    section_id = lax.axis_index("section")
    joint_id = lax.axis_index("joint")
    block_len = encoder_rows.shape[1]
    utterances = label_ids.shape[0]
    places = label_ids.shape[1] + 1
    own_rows = encoder_rows[0].astype(jnp.float32)
    normed_in = layer_norm(own_rows)[0].astype(jnp.bfloat16)
    gathered = lax.all_gather(normed_in, "section", axis=0, tiled=True)
    pre_hidden = jnp.dot(gathered, up_weight, preferred_element_type=jnp.float32)
    hidden = jax.nn.silu(pre_hidden).astype(jnp.bfloat16)
    encoded = own_rows + lax.psum_scatter(
        0.5 * jnp.dot(hidden, down_weight, preferred_element_type=jnp.float32),
        "section",
        scatter_dimension=0,
        tiled=True,
    )
    unit_rows, inv_scale = layer_norm(encoded)
    frame_part = jnp.dot(
        unit_rows.astype(jnp.bfloat16), encoder_proj, preferred_element_type=jnp.float32
    ).astype(jnp.bfloat16)
    order_iota = jnp.arange(utterances, dtype=jnp.int32)
    inverse = jnp.zeros((utterances,), jnp.int32).at[owner_index].set(order_iota)
    own_utterance = inverse[joint_id]
    owner_frames = route_owner(frame_part, owner_index, joint_id, joint_count)
    context = jnp.concatenate([jnp.zeros((utterances, 1), jnp.int32), label_ids], axis=1)
    vocab_rows = embedding.shape[0]
    vocab_ids = joint_id * vocab_rows + jnp.arange(vocab_rows, dtype=jnp.int32)

    def label_term(start_row, row_count):
        number = row_count // places
        wanted = context[inverse].reshape(number * places)
        selector = (wanted[:, None] == vocab_ids[None, :]).astype(jnp.bfloat16)
        return jnp.dot(selector, embedding, preferred_element_type=jnp.float32)

    looked = lax.psum_scatter(
        label_term(jnp.int32(0), places * lax.axis_size("joint")).astype(jnp.bfloat16),
        "joint",
        scatter_dimension=0,
        tiled=True,
    ).astype(jnp.float32)
    previous = jnp.concatenate([looked[:1], looked[:-1]], axis=0)
    pred_act = jnp.maximum(conv_taps[0] * previous + conv_taps[1] * looked, 0.0).astype(
        jnp.bfloat16
    )
    pred_rows = jnp.dot(pred_act, decoder_proj, preferred_element_type=jnp.float32)
    label_here = label_ids[own_utterance]
    frames_used = frame_lengths[own_utterance]
    labels_used = label_lengths[own_utterance]
    joined, posterior, blank_score, label_score = joint_forward(
        owner_frames, pred_rows, label_here, output_proj, output_bias
    )
    frame_ids = section_id * block_len + jnp.arange(block_len, dtype=jnp.int32)
    active = frame_ids < frames_used
    transfer = block_matrix(blank_score, label_score, active)
    place_iota = jnp.arange(places, dtype=jnp.int32)
    start_vec = jnp.where(place_iota == 0, 0.0, NEG_BIG)
    finish_vec = jnp.where(place_iota == labels_used, 0.0, NEG_BIG)

    def forward_turn(turn_index, carried):
        passed = from_behind(log_apply(transfer, carried), "section", 1)
        return jnp.where(section_id == 0, start_vec, passed)

    incoming = lax.fori_loop(0, section_count - 1, forward_turn, start_vec)

    def backward_turn(turn_index, carried):
        passed = from_behind(log_apply_back(transfer, carried), "section", -1)
        return jnp.where(section_id == section_count - 1, finish_vec, passed)

    leaving = lax.fori_loop(0, section_count - 1, backward_turn, finish_vec)

    def block_out(blank_in, label_in):
        return run_block(incoming, blank_in, label_in, active)

    end_alpha, pullback = jax.vjp(block_out, blank_score, label_score)
    logprob = jax.nn.logsumexp(end_alpha + leaving)
    blank_grad, label_grad = pullback(-jnp.exp(end_alpha + leaving - logprob))
    frame_part_grad, pred_part = joint_backward(
        blank_grad, label_grad, label_here, joined, posterior, output_proj
    )
    part_grad = route_holder(frame_part_grad, inverse, joint_id, joint_count)
    unit_grad = lax.dot_general(
        part_grad, encoder_proj, (((1,), (1,)), ((), ())), preferred_element_type=jnp.float32
    )
    first_mean = jnp.mean(unit_grad, axis=-1, keepdims=True)
    second_mean = jnp.mean(unit_grad * unit_rows, axis=-1, keepdims=True)
    row_grad = (inv_scale * (unit_grad - first_mean - unit_rows * second_mean)).astype(jnp.bfloat16)
    grad_all = lax.all_gather(row_grad, "section", axis=0, tiled=True)
    hidden_grad = 0.5 * lax.dot_general(
        grad_all, down_weight, (((1,), (1,)), ((), ())), preferred_element_type=jnp.float32
    )
    gate_sigmoid = jax.nn.sigmoid(pre_hidden)
    pre_grad = (hidden_grad * gate_sigmoid * (1.0 + pre_hidden * (1.0 - gate_sigmoid))).astype(
        jnp.bfloat16
    )
    up_part = lax.dot_general(
        gathered, pre_grad, (((0,), (0,)), ((), ())), preferred_element_type=jnp.float32
    )
    down_part = 0.5 * lax.dot_general(
        hidden, grad_all, (((0,), (0,)), ((), ())), preferred_element_type=jnp.float32
    )
    up_sum, down_sum = (
        lax.psum_scatter(
            up_part.astype(jnp.bfloat16), "joint", scatter_dimension=0, tiled=True
        ).astype(jnp.float32),
        lax.psum_scatter(
            down_part.astype(jnp.bfloat16), "joint", scatter_dimension=1, tiled=True
        ).astype(jnp.float32),
    )
    pred_sum = lax.psum_scatter(pred_part[None], "section", scatter_dimension=2, tiled=True)
    return (row_grad[None], up_sum, down_sum, pred_sum)


def solution(mesh):
    return jax.shard_map(
        on_device,
        mesh=mesh,
        in_specs=(
            P("joint", "section", None),
            P(None, "section"),
            P("section", None),
            P(),
            P("joint", None),
            P(),
            P(),
            P(),
            P(),
            P(),
            P(),
            P(),
            P(),
        ),
        out_specs=(
            P("joint", "section", None),
            P("joint", "section"),
            P("section", "joint"),
            P("joint", None, "section"),
        ),
        check_vma=False,
    )
```

profile of v0, /device:TPU:2, one launch (start us, length us, event | category | flops | bytes accessed | tf_op | source)
XLA Modules:
  0.0 2108.3 jit_solution(6235568972007815648)
XLA Ops:
  12.7 48.0 %all-gather.3.cloned.1.call-done = bf16[1024,1536]{1,0:T(8,128)(2,1)} async-done(((bf16[128,1536]{1,0:T(8,128)(2,1)}), bf16[1024,1536]{1,0:T(8,128)(2,1)}) %all-gather.3.cloned.1.call-update) | async-done | bytes 3145744 | tf_op jit(solution)/shard_map/all_gather | solution.py:191
  65.7 4.5 convolution_multiply_fusion
  86.9 57.3 %reduce-scatter.7.cloned.1.call-done = f32[128,1536]{1,0:T(8,128)} async-done(((f32[1024,1536]{1,0:T(8,128)}), f32[128,1536]{1,0:T(8,128)}) %reduce-scatter.7.cloned.1.call-update) | async-done | bytes 786448 | tf_op jit(solution)/shard_map/reduce_scatter | solution.py:194
  179.8 5.0 collective-permute-done.8
  232.5 6.8 broadcast_in_dim.223
  246.4 9.4 exponential_reduce_fusion.3
  255.9 9.8 reshape.609
  266.7 5.5 gather_fusion.31
  275.0 308.2 %while.74 = (s32[]{:T(128)}, f32[4,4]{1,0:T(4,128)S(1)}, pred[128]{0:T(512)(128)(4,1)S(1)}, f32[128,4]{1,0:T(8,128)S(1)}, f32[128,3]{1,0:T(8,128)}, /*index=5*/s32[]{:T(128)}, f32[]{:T(128)}, f32[1]{0:T(128)}) while((s32[]{:T(128)}, f32[4,4]{1,0:T(4,128)S(1)}, pred[128]{0:T(512)(128)(4,1)S(1)}, f32[128,4]{1,0:T(8,128)S(1)}, ...), condition=%wide.region_12.13_spmd, body=%wide.region_8.0_spmd.sunk | while | flops 476 | bytes 1144 | solution.py:68
  583.2 39.8 %while.75 = (s32[]{:T(128)}, f32[4]{0:T(128)S(1)}, pred[]{:T(512)}, f32[4,4]{1,0:T(4,128)S(1)}, s32[]{:T(128)}) while((s32[]{:T(128)}, f32[4]{0:T(128)S(1)}, pred[]{:T(512)}, f32[4,4]{1,0:T(4,128)S(1)}, s32[]{:T(128)}) %tuple.157), condition=%wide.region_16.17_spmd.clone, body=%wide.region_13.16_spmd.clone.sunk | while | flops 110 | bytes 486 | solution.py:246
  610.0 4.7 collective-permute-start
  616.3 5.4 collective-permute-start
  623.0 567.5 %while.78 = (s32[]{:T(128)}, f32[4]{0:T(128)S(1)}, f32[128,4,4]{2,1,0:T(4,128)}, pred[128,4]{1,0:T(8,128)(4,1)}, f32[128,4]{1,0:T(8,128)S(1)}, /*index=5*/pred[1...) while((s32[]{:T(128)}, f32[4]{0:T(128)S(1)}, ...), condition=%wide.region_21.22_spmd.clone.clone, body=%wide.region_17.21_spmd.clone.clone.sunk | while | flops 296 | bytes 5132 | solution.py:52
  1190.5 53.7 %while.76 = (s32[]{:T(128)}, f32[4]{0:T(128)S(1)}, pred[]{:T(512)}, f32[4,4]{1,0:T(4,128)S(1)}, s32[]{:T(128)}, /*index=5*/s32[]{:T(128)}) while((s32[]{:T(128)}, f32[4]{0:T(128)S(1)}, pred[]{:T(512)}, f32[4,4]{1,0:T(4,128)S(1)}, s32[]{:T(128)}, /*index=5*/s32[]{:T(128)}) %tuple.183), condition=%wide.region_25.26_spmd.clone, body=%wide.region_22.25_spmd.clone.sunk | while | flops 110 | bytes 498 | solution.py:252
  1192.0 5.6 collective-permute-done.1
  1199.7 5.6 collective-permute-done.1
  1207.5 5.6 collective-permute-done.1
  1215.3 5.6 collective-permute-done.1
  1223.1 5.4 collective-permute-done.1
  1230.6 5.4 collective-permute-done.1
  1238.1 5.4 collective-permute-done.1
  1247.4 484.2 %while.77 = (s32[]{:T(128)}, f32[4]{0:T(128)S(1)}, f32[128,4]{1,0:T(8,128)S(1)}, f32[128,3]{1,0:T(8,128)S(1)}, pred[128]{0:T(512)(128)(4,1)S(1)}, /*index=5*/pre...) while((s32[]{:T(128)}, f32[4]{0:T(128)S(1)}, ...), condition=%wide.region_33.34_spmd.clone, body=%wide.region_28.33_spmd.clone.sunk | while | flops 133 | bytes 553 | solution.py:52
  1731.9 12.4 fusion.31
  1766.4 4.6 collective-permute-done.20
  1788.3 5.2 collective-permute-start.24
  1822.1 5.0 collective-permute-start.29
  1843.2 49.4 %all-gather.5.cloned.1.call-done = bf16[1024,1536]{1,0:T(8,128)(2,1)} async-done(((bf16[128,1536]{1,0:T(8,128)(2,1)}), bf16[1024,1536]{1,0:T(8,128)(2,1)}) %all-gather.5.cloned.1.call-update) | async-done | bytes 3145744 | tf_op jit(solution)/shard_map/all_gather | solution.py:270
  1892.6 5.3 fusion.30
  1898.0 7.8 convolution_convert_fusion
  1905.8 25.1 %reduce-scatter.13.cloned.1.call-done = f32[80,4]{1,0:T(8,128)} async-done(((f32[640,4]{1,0:T(8,128)}), f32[80,4]{1,0:T(8,128)}) %reduce-scatter.13.cloned.1.call-update) | async-done | bytes 1296
  1932.3 82.1 %reduce-scatter.11.cloned.1.call-done = bf16[384,48]{0,1:T(8,128)(2,1)} async-done(((bf16[384,1536]{0,1:T(8,128)(2,1)}), bf16[384,48]{0,1:T(8,128)(2,1)}) %reduce-scatter.11.cloned.1.call-update) | async-done | bytes 36880 | tf_op jit(solution)/shard_map/reduce_scatter | solution.py:288
  2015.8 83.2 %reduce-scatter.9.cloned.1.call-done = bf16[48,384]{1,0:T(8,128)(2,1)} async-done(((bf16[1536,384]{1,0:T(8,128)(2,1)}), bf16[48,384]{1,0:T(8,128)(2,1)}) %reduce-scatter.9.cloned.1.call-update) | async-done | bytes 36880 | tf_op jit(solution)/shard_map/reduce_scatter | solution.py:285
  (4265 shorter events, 1567.4 us)
Async XLA Ops:
  8.0 52.7 %all-gather.3.cloned.1.call-start = ((), (), s32[]{:S(2)}) async-start(), calls=%async_computation.4 | async-start | bytes 3538944 | tf_op jit(solution)/shard_map/all_gather | solution.py:191
  12.6 131.5 %reduce-scatter.7.cloned.1.call-start = ((), (), s32[]{:S(2)}) async-start(), calls=%async_computation.5 | async-start | bytes 7077888 | tf_op jit(solution)/shard_map/reduce_scatter | solution.py:194
  70.2 170.3 %all-reduce.5.cloned.1.call-start = ((), (), s32[]{:S(2)}) async-start(), calls=%async_computation.10 | async-start | bytes 327680
  74.8 1817.9 %all-gather.5.cloned.1.call-start = ((), (), s32[]{:S(2)}) async-start(), calls=%async_computation.6 | async-start | bytes 3538944 | tf_op jit(solution)/shard_map/all_gather | solution.py:270
  149.0 7.0 collective-permute-start.3
  160.2 7.8 collective-permute-start.5
  168.0 8.9 collective-permute-start.6
  178.4 6.4 collective-permute-start.8
  184.8 7.0 collective-permute-start.9
  191.9 6.3 collective-permute-start.10
  200.3 7.8 collective-permute-start.12
  213.7 6.9 collective-permute-start.14
  222.2 19.1 collective-permute-start.15
  610.0 6.0 collective-permute-start
  616.3 6.7 collective-permute-start
  1190.7 6.9 collective-permute-start.1
  1198.4 6.9 collective-permute-start.1
  1206.2 6.9 collective-permute-start.1
  1214.0 6.9 collective-permute-start.1
  1221.8 6.7 collective-permute-start.1
  1229.3 6.7 collective-permute-start.1
  1236.8 6.7 collective-permute-start.1
  1752.1 6.8 collective-permute-start.18
  1763.1 7.8 collective-permute-start.20
  1780.2 8.0 collective-permute-start.23
  1788.3 9.5 collective-permute-start.24
  1797.8 6.5 collective-permute-start.25
  1808.3 8.0 collective-permute-start.27
  1822.1 8.6 collective-permute-start.29
  1842.2 88.7 %reduce-scatter.13.cloned.1.call-start = ((), (), s32[]{:S(2)}) async-start(), calls=%async_computation.9 | async-start | bytes 368640
  1843.2 171.3 %reduce-scatter.11.cloned.1.call-start = ((), (), s32[]{:S(2)}) async-start(), calls=%async_computation.8 | async-start | bytes 1216512 | tf_op jit(solution)/shard_map/reduce_scatter | solution.py:288
  1897.9 201.1 %reduce-scatter.9.cloned.1.call-start = ((), (), s32[]{:S(2)}) async-start(), calls=%async_computation.7 | async-start | bytes 1216512 | tf_op jit(solution)/shard_map/reduce_scatter | solution.py:285
  (47 other events, 2084.4 us)
Sparse Core Ops, SparseCore 0:
  12.8 47.9 all-gather.2
  70.3 73.7 reduce-scatter.6
  1842.3 50.2 all-gather.4
  1895.0 35.8 reduce-scatter.12
  1934.6 79.7 reduce-scatter.10
  2018.1 80.8 reduce-scatter.8
Sparse Core Ops, SparseCore 1:
  74.9 107.8 all-reduce.4
where the time goes:
time: 2140 us; the launch traced here: 2110 us
  other arithmetic  813 us (38%)
  local copies, waits for them, and re-layouts  667 us (31%)
  waiting for transfers between devices  437 us (20%)
  starting transfers between devices  79.3 us (4%)
  between operations  60.3 us (3%)
  matrix products  46.8 us (2%)
    dynamic_slice x384, local copies, waits for them, and re-layouts, block_matrix(): lax.scan(block_one_frame, identity_map, (blank_score, label_score, active))  219 us
    another operation x386, local copies, waits for them, and re-layouts  187 us
    dynamic_update_slice x512, local copies, waits for them, and re-layouts, run_block(): lax.scan(run_one_frame, vector, (blank_score, label_score, active))[0]  173 us
    broadcast_in_dim x130, other arithmetic, run_block(): lax.scan(run_one_frame, vector, (blank_score, label_score, active))[0]  171 us
    reduce_sum x128, other arithmetic, lower_paths(): partial_sums[:, None] - partial_sums[None, :]  112 us
    dynamic_update_slice x128, other arithmetic, run_block(): lax.scan(run_one_frame, vector, (blank_score, label_score, active))[0]  84.6 us
    add_any x128, other arithmetic, advance(): vector[None, :]  84.1 us
    reduce_scatter x1, waiting for transfers between devices, on_device(): lax.psum_scatter(up_part.astype(jnp.bfloat16), 'joint', scatter_dimension...  83.2 us

commit v1 on v0

--- a/solution.py
+++ b/solution.py
@@ -267,7 +267,9 @@
     first_mean = jnp.mean(unit_grad, axis=-1, keepdims=True)
     second_mean = jnp.mean(unit_grad * unit_rows, axis=-1, keepdims=True)
     row_grad = (inv_scale * (unit_grad - first_mean - unit_rows * second_mean)).astype(jnp.bfloat16)
-    grad_all = lax.all_gather(row_grad, "section", axis=0, tiled=True)
+    grad_all = jnp.concatenate(
+        lax.all_to_all(jnp.stack([row_grad] * lax.axis_size("section")), "section", 0, 0), axis=0
+    )
     hidden_grad = 0.5 * lax.dot_general(
         grad_all, down_weight, (((1,), (1,)), ((), ())), preferred_element_type=jnp.float32
     )

time: 2140 us -> 2190 us (1.023)
  other arithmetic: 813 us -> 836 us
    all_to_all x0 -> x1, waiting for transfers between devices: none -> 76.5 us  [on_device(): lax.all_to_all(jnp.stack([row_grad] * lax.axis_size('section')), 'section...]
    all_gather x1 -> x0, waiting for transfers between devices: 49.4 us -> none  [on_device(): grad_all = lax.all_gather(row_grad, 'section', axis=0, tiled=True)]
    unnamed x9 -> x8, waiting for transfers between devices: 25.2 us -> 0.15 us
    another operation x386 -> x387, local copies, waits for them, and re-layouts: 187 us -> 189 us
where the time goes in v1:
time: 2190 us; the launch traced here: 2150 us
  other arithmetic  836 us (38%)
  local copies, waits for them, and re-layouts  686 us (31%)
  waiting for transfers between devices  427 us (19%)
  starting transfers between devices  90.1 us (4%)
  between operations  59.8 us (3%)
  matrix products  46.8 us (2%)
    dynamic_slice x384, local copies, waits for them, and re-layouts, block_matrix(): lax.scan(block_one_frame, identity_map, (blank_score, label_score, active))  237 us
    another operation x386, local copies, waits for them, and re-layouts  187 us
    dynamic_update_slice x512, local copies, waits for them, and re-layouts, run_block(): lax.scan(run_one_frame, vector, (blank_score, label_score, active))[0]  173 us
    broadcast_in_dim x130, other arithmetic, run_block(): lax.scan(run_one_frame, vector, (blank_score, label_score, active))[0]  171 us
    reduce_sum x128, other arithmetic, lower_paths(): partial_sums[:, None] - partial_sums[None, :]  112 us
    select_n x128, other arithmetic, block_one_frame(): return (jnp.where(live_flag, moved, carried), None)  96.1 us
    dynamic_update_slice x128, other arithmetic, run_block(): lax.scan(run_one_frame, vector, (blank_score, label_score, active))[0]  84.6 us
    add_any x128, other arithmetic, advance(): vector[None, :]  84.1 us

profile of v1, /device:TPU:2, one launch (start us, length us, event | category | flops | bytes accessed | tf_op | source)
XLA Modules:
  0.0 2151.8 jit_solution(12089889038722543542)
XLA Ops:
  12.7 48.0 %all-gather.2.cloned.1.call-done = bf16[1024,1536]{1,0:T(8,128)(2,1)} async-done(((bf16[128,1536]{1,0:T(8,128)(2,1)}), bf16[1024,1536]{1,0:T(8,128)(2,1)}) %all-gather.2.cloned.1.call-update) | async-done | bytes 3145744 | tf_op jit(solution)/shard_map/all_gather | solution.py:191
  65.7 4.5 convolution_multiply_fusion
  86.8 57.3 %reduce-scatter.7.cloned.1.call-done = f32[128,1536]{1,0:T(8,128)} async-done(((f32[1024,1536]{1,0:T(8,128)}), f32[128,1536]{1,0:T(8,128)}) %reduce-scatter.7.cloned.1.call-update) | async-done | bytes 786448 | tf_op jit(solution)/shard_map/reduce_scatter | solution.py:194
  178.9 5.6 collective-permute-done.8
  231.5 6.8 broadcast_in_dim.223
  245.4 9.4 exponential_reduce_fusion.3
  254.8 9.8 reshape.614
  265.6 5.5 gather_fusion.31
  273.9 337.9 %while.74 = (s32[]{:T(128)}, f32[4,4]{1,0:T(4,128)S(1)}, pred[128]{0:T(512)(128)(4,1)S(1)}, f32[128,4]{1,0:T(8,128)S(1)}, f32[128,3]{1,0:T(8,128)}, /*index=5*/s32[]{:T(128)}, f32[]{:T(128)}, f32[1]{0:T(128)}) while((s32[]{:T(128)}, f32[4,4]{1,0:T(4,128)S(1)}, pred[128]{0:T(512)(128)(4,1)S(1)}, f32[128,4]{1,0:T(8,128)S(1)}, ...), condition=%wide.region_12.13_spmd, body=%wide.region_8.0_spmd.sunk | while | flops 476 | bytes 1144 | solution.py:68
  611.7 39.8 %while.75 = (s32[]{:T(128)}, f32[4]{0:T(128)S(1)}, pred[]{:T(512)}, f32[4,4]{1,0:T(4,128)S(1)}, s32[]{:T(128)}) while((s32[]{:T(128)}, f32[4]{0:T(128)S(1)}, pred[]{:T(512)}, f32[4,4]{1,0:T(4,128)S(1)}, s32[]{:T(128)}) %tuple.157), condition=%wide.region_16.17_spmd.clone, body=%wide.region_13.16_spmd.clone.sunk | while | flops 110 | bytes 486 | solution.py:246
  638.5 4.8 collective-permute-start
  644.9 5.4 collective-permute-start
  651.6 582.1 %while.78 = (s32[]{:T(128)}, f32[4]{0:T(128)S(1)}, f32[128,4,4]{2,1,0:T(4,128)}, pred[128,4]{1,0:T(8,128)(4,1)}, f32[128,4]{1,0:T(8,128)S(1)}, /*index=5*/pred[1...) while((s32[]{:T(128)}, f32[4]{0:T(128)S(1)}, ...), condition=%wide.region_21.22_spmd.clone.clone, body=%wide.region_17.21_spmd.clone.clone.sunk | while | flops 296 | bytes 5132 | solution.py:52
  1233.7 53.7 %while.76 = (s32[]{:T(128)}, f32[4]{0:T(128)S(1)}, pred[]{:T(512)}, f32[4,4]{1,0:T(4,128)S(1)}, s32[]{:T(128)}, /*index=5*/s32[]{:T(128)}) while((s32[]{:T(128)}, f32[4]{0:T(128)S(1)}, pred[]{:T(512)}, f32[4,4]{1,0:T(4,128)S(1)}, s32[]{:T(128)}, /*index=5*/s32[]{:T(128)}) %tuple.181), condition=%wide.region_25.26_spmd.clone, body=%wide.region_22.25_spmd.clone.sunk | while | flops 110 | bytes 498 | solution.py:252
  1235.1 5.6 collective-permute-done.1
  1242.9 5.6 collective-permute-done.1
  1250.7 5.6 collective-permute-done.1
  1258.5 5.6 collective-permute-done.1
  1266.3 5.4 collective-permute-done.1
  1273.8 5.4 collective-permute-done.1
  1281.3 5.4 collective-permute-done.1
  1290.6 484.2 %while.77 = (s32[]{:T(128)}, f32[4]{0:T(128)S(1)}, f32[128,4]{1,0:T(8,128)S(1)}, f32[128,3]{1,0:T(8,128)S(1)}, pred[128]{0:T(512)(128)(4,1)S(1)}, /*index=5*/pre...) while((s32[]{:T(128)}, f32[4]{0:T(128)S(1)}, ...), condition=%wide.region_33.34_spmd.clone, body=%wide.region_28.33_spmd.clone.sunk | while | flops 133 | bytes 553 | solution.py:52
  1775.1 12.3 fusion.31
  1809.8 4.3 collective-permute-done.20
  1831.7 5.2 collective-permute-start.24
  1865.6 5.0 collective-permute-start.29
  1887.0 9.8 all-to-all-start
  1897.9 76.5 %all-to-all-done = bf16[8,128,1536]{2,1,0:T(8,128)(2,1)} async-done(((bf16[8,128,1536]{2,1,0:T(8,128)(2,1)}), bf16[8,128,1536]{2,1,0:T(8,128)(2,1)}, u32[]{:S(2)}, u32[]{:S(2)}) %all-to-all-start) | async-done | bytes 3145760 | tf_op jit(solution)/shard_map/all_to_all | solution.py:271
  1974.4 5.4 fusion.30
  1979.8 7.8 convolution_convert_fusion
  1989.1 69.2 %reduce-scatter.11.cloned.1.call-done = bf16[384,48]{0,1:T(8,128)(2,1)} async-done(((bf16[384,1536]{0,1:T(8,128)(2,1)}), bf16[384,48]{0,1:T(8,128)(2,1)}) %reduce-scatter.11.cloned.1.call-update) | async-done | bytes 36880 | tf_op jit(solution)/shard_map/reduce_scatter | solution.py:290
  2059.7 83.1 %reduce-scatter.9.cloned.1.call-done = bf16[48,384]{1,0:T(8,128)(2,1)} async-done(((bf16[1536,384]{1,0:T(8,128)(2,1)}), bf16[48,384]{1,0:T(8,128)(2,1)}) %reduce-scatter.9.cloned.1.call-update) | async-done | bytes 36880 | tf_op jit(solution)/shard_map/reduce_scatter | solution.py:287
  (4275 shorter events, 1612.2 us)
Async XLA Ops:
  8.0 52.7 %all-gather.2.cloned.1.call-start = ((), (), s32[]{:S(2)}) async-start(), calls=%async_computation.5 | async-start | bytes 3538944 | tf_op jit(solution)/shard_map/all_gather | solution.py:191
  12.7 131.5 %reduce-scatter.7.cloned.1.call-start = ((), (), s32[]{:S(2)}) async-start(), calls=%async_computation.6 | async-start | bytes 7077888 | tf_op jit(solution)/shard_map/reduce_scatter | solution.py:194
  70.2 169.3 %all-reduce.5.cloned.1.call-start = ((), (), s32[]{:S(2)}) async-start(), calls=%async_computation.10 | async-start | bytes 327680
  149.0 6.9 collective-permute-start.3
  160.2 7.8 collective-permute-start.5
  168.0 8.5 collective-permute-start.6
  178.1 6.4 collective-permute-start.8
  184.5 7.0 collective-permute-start.9
  191.6 6.3 collective-permute-start.10
  199.9 7.8 collective-permute-start.12
  213.3 6.9 collective-permute-start.14
  221.8 18.4 collective-permute-start.15
  638.5 6.1 collective-permute-start
  644.9 6.7 collective-permute-start
  1233.8 6.9 collective-permute-start.1
  1241.6 6.9 collective-permute-start.1
  1249.4 6.9 collective-permute-start.1
  1257.2 6.9 collective-permute-start.1
  1265.0 6.7 collective-permute-start.1
  1272.5 6.7 collective-permute-start.1
  1280.0 6.7 collective-permute-start.1
  1795.3 6.8 collective-permute-start.18
  1806.3 7.8 collective-permute-start.20
  1823.5 8.2 collective-permute-start.23
  1831.7 9.5 collective-permute-start.24
  1841.3 6.5 collective-permute-start.25
  1851.9 8.0 collective-permute-start.27
  1865.6 8.6 collective-permute-start.29
  1887.0 87.3 %all-to-all-start = ((bf16[8,128,1536]{2,1,0:T(8,128)(2,1)}), bf16[8,128,1536]{2,1,0:T(8,128)(2,1)}, u32[]{:S(2)}, u32[]{:S(2)}) async-start(bf16[8,128,1536]{2,1,0:T(8,128)(2,1)} %stack.2), calls=%async_computation.1 | async-start | bytes 6291456 | tf_op jit(solution)/shard_map/all_to_all | solution.py:271
  1896.8 90.8 %reduce-scatter.13.cloned.1.call-start = ((), (), s32[]{:S(2)}) async-start(), calls=%async_computation.9 | async-start | bytes 368640
  1897.8 160.5 %reduce-scatter.11.cloned.1.call-start = ((), (), s32[]{:S(2)}) async-start(), calls=%async_computation.8 | async-start | bytes 1216512 | tf_op jit(solution)/shard_map/reduce_scatter | solution.py:290
  1979.8 163.1 %reduce-scatter.9.cloned.1.call-start = ((), (), s32[]{:S(2)}) async-start(), calls=%async_computation.7 | async-start | bytes 1216512 | tf_op jit(solution)/shard_map/reduce_scatter | solution.py:287
  (52 other events, 2181.1 us)
Sparse Core Ops, SparseCore 0:
  12.8 47.9 all-gather.1
  70.4 73.7 reduce-scatter.6
  1900.2 46.8 reduce-scatter.12
  1979.9 78.4 reduce-scatter.10
  2062.0 80.7 reduce-scatter.8
Sparse Core Ops, SparseCore 1:
  74.9 107.9 all-reduce.4
